TPU v7x, 512 devices: a whole 4x4x16 slice. The times are simulated.
512 devices in a mesh: dp: 8 (over z_hi, core), dom: 64 (over x, z_lo, y).
Axes of the slice: x: 4, y: 4, z: 16 (z_hi: 4, z_lo: 4; z = z_hi * 4 + z_lo), core: 2. Of those that a mesh axis runs over, the one named last changes fastest.
Arguments:
- density: bfloat16 [8, 64, 512, 256], P('dp', None, 'dom'), may hold values from -6 to 6
- upstream: bfloat16 [8, 64, 512, 256], P('dp', None, 'dom'), may hold values from -6 to 6
- spectral_weight: float32 [2048, 64], P(('dp', 'dom')), may hold values from -0.5 to 0.5
- moment_one: float32 [2048, 64], P(('dp', 'dom')), may hold values from -128 to 128
- moment_two: float32 [2048, 64], P(('dp', 'dom')), may hold values from 256 to 4096
- skip_weight: bfloat16 [64, 64], replicated, may hold values from -0.75 to 0.75
- skip_bias: float32 [64], replicated, may hold values from -3 to 3
- mode_counts: int32 [8], replicated, may hold values from 8 to 16, as said below
Outputs:
- input_grad: bfloat16 [8, 64, 512, 256], P('dp', None, 'dom')
- new_weight: float32 [2048, 64], P(('dp', 'dom'))
- new_moment_one: float32 [2048, 64], P(('dp', 'dom'))
- new_moment_two: float32 [2048, 64], P(('dp', 'dom'))
Inputs may be any that keep to these rules, and one draw needn't show every extreme that they name: `mode_counts`: some entry equals 16.
All inputs are finite; a program needn't handle non-finite values.
Results may differ from a plain program's by a relative error of at most 0.0053.
Values may be sent and summed in bfloat16 or wider, within the bound.
No kernel may reach another device: no remote copies, remote signals or barrier semaphores. Data moves between devices by JAX's collectives and lax.ppermute only.
A program may use at most 64 MiB of HBM per device.

v0:
```python
import math
import jax
import jax.numpy as jnp
from jax import lax
from jax.sharding import PartitionSpec as P

MODES = 16
STEP = 10
learn_rate = 0.01
beta_first = 0.9
beta_second = 0.95
decay_rate = 0.1
epsilon = 1e-08


def joined_along(tiles, dim):
    dims = list(tiles.shape[1:])
    dims[dim] *= tiles.shape[0]
    return jnp.moveaxis(tiles, 0, dim).reshape(dims)


def copy_for_each(shard, axis):
    copies = jnp.broadcast_to(shard, (lax.axis_size(axis), *shard.shape))
    return lax.all_to_all(copies, axis, split_axis=0, concat_axis=0, tiled=True)


def collect(shard, axis, dim):
    return joined_along(copy_for_each(shard, axis), dim)


def in_one_piece(arrays, axis, split_dim, concat_dim, along):
    both = jnp.concatenate(arrays, axis=along)
    result, at, done = (
        lax.all_to_all(both, axis, split_axis=split_dim, concat_axis=concat_dim, tiled=True),
        0,
        [],
    )
    for a in arrays:
        done.append(lax.slice_in_dim(result, at, at + a.shape[along], axis=along))
        at += a.shape[along]
    return tuple(done)


def split_up(shard, dim, length):
    dims = shard.shape
    tiles = shard.reshape(*dims[:dim], length, dims[dim] // length, *dims[dim + 1 :])
    return jnp.moveaxis(tiles, dim, 0)


def sum_at_owner(shard, axis, dim):
    tiles = split_up(shard, dim, lax.axis_size(axis))
    arrived = lax.all_to_all(tiles, axis, split_axis=0, concat_axis=0, tiled=True)
    return arrived.astype(jnp.float32).sum(axis=0)


def summed_on_arrival(shard, axis, dim):
    length = lax.axis_size(axis)
    tiles = lax.all_to_all(split_up(shard, dim, length), axis, 0, 0, tiled=True)
    return jnp.sum(tiles, axis=0)


def axis_parts(count_xdim):
    freq_list = jnp.arange(MODES, dtype=jnp.int32)
    cell_list = jnp.arange(count_xdim, dtype=jnp.int32)
    phases = (
        jnp.mod(freq_list[:, None] * cell_list[None, :], count_xdim).astype(jnp.float32)
        / count_xdim
    )
    angles = 2.0 * math.pi * phases
    scaling = 1.0 / math.sqrt(count_xdim)
    return (
        (jnp.cos(angles) * scaling).astype(jnp.bfloat16),
        (jnp.sin(angles) * scaling).astype(jnp.bfloat16),
    )


def doubling_table():
    return jnp.where(jnp.arange(MODES, dtype=jnp.int32) > 0, 2.0, 1.0).astype(jnp.float32)


def gelu_slope(values):
    cumulative = 0.5 * (1.0 + lax.erf(values * 0.7071067811865476))
    bell_curve = jnp.exp(-0.5 * values * values) * 0.3989422804014327
    return cumulative + values * bell_curve


def forward_parts(field, cosines, sines):
    real_part = jnp.einsum("scxl,fx->slcf", field, cosines, preferred_element_type=jnp.float32)
    imag_part = -jnp.einsum("scxl,fx->slcf", field, sines, preferred_element_type=jnp.float32)
    return (real_part, imag_part)


def inverse_cells(values_real, values_imag, cosines, sines):
    first = jnp.einsum("slcf,fx->scxl", values_real, cosines, preferred_element_type=jnp.float32)
    second = jnp.einsum("slcf,fx->scxl", values_imag, sines, preferred_element_type=jnp.float32)
    return (first - second).astype(jnp.bfloat16)


def on_device(
    density, upstream, spectral_weight, moment_one, moment_two, skip_weight, skip_bias, mode_counts
):
    samples, channels, slab_rows, line_count = density.shape
    count_xdim = slab_rows * lax.axis_size("dom")
    cosines, sines = axis_parts(count_xdim)
    doubling = doubling_table()
    doubling_low = doubling.astype(jnp.bfloat16)
    counts_here = lax.dynamic_slice_in_dim(mode_counts, lax.axis_index("dp") * samples, samples, 0)
    keep_modes = (jnp.arange(MODES, dtype=jnp.int32)[None, :] < counts_here[:, None]).astype(
        jnp.float32
    )
    keep_wide = keep_modes[:, None, None, :]
    weight_short = spectral_weight.astype(jnp.bfloat16)
    weight_low = lax.all_gather(weight_short, ("dp", "dom"), axis=0, tiled=True)
    weight_low = weight_low.reshape(2, MODES, channels, channels)
    weight_real = weight_low[0]
    weight_imag = weight_low[1]
    density_lines, upstream_lines = in_one_piece((density, upstream), "dom", 3, 2, 0)
    real_part, imag_part = forward_parts(density_lines, cosines, sines)
    spec_real = real_part.astype(jnp.bfloat16)
    spec_imag = imag_part.astype(jnp.bfloat16)
    form = "slcf,fco->slof"
    mixed_real = jnp.einsum(
        form, spec_real, weight_real, preferred_element_type=jnp.float32
    ) - jnp.einsum(form, spec_imag, weight_imag, preferred_element_type=jnp.float32)
    mixed_imag = jnp.einsum(
        form, spec_imag, weight_real, preferred_element_type=jnp.float32
    ) + jnp.einsum(form, spec_real, weight_imag, preferred_element_type=jnp.float32)
    mixed_real = (mixed_real * keep_wide).astype(jnp.bfloat16) * doubling_low
    mixed_imag = (mixed_imag * keep_wide).astype(jnp.bfloat16) * doubling_low
    back_lines = inverse_cells(mixed_real, mixed_imag, cosines, sines)
    back_rows = lax.optimization_barrier(back_lines)
    skip_part = jnp.einsum(
        "oc,scxl->soxl", skip_weight, density_lines, preferred_element_type=jnp.float32
    )
    before = back_rows.astype(jnp.float32) + skip_part + skip_bias[None, :, None, None]
    gate_lines = (upstream_lines.astype(jnp.float32) * gelu_slope(before)).astype(jnp.bfloat16)
    grad_real, grad_imag = forward_parts(gate_lines, cosines, sines)
    scale = keep_wide * doubling
    grad_real = (grad_real * scale).astype(jnp.bfloat16)
    grad_imag = (grad_imag * scale).astype(jnp.bfloat16)
    outer = "slof,slcf->fco"
    part_real = jnp.einsum(
        outer, grad_real, spec_real, preferred_element_type=jnp.float32
    ) + jnp.einsum(outer, grad_imag, spec_imag, preferred_element_type=jnp.float32)
    part_imag = jnp.einsum(
        outer, grad_imag, spec_real, preferred_element_type=jnp.float32
    ) - jnp.einsum(outer, grad_real, spec_imag, preferred_element_type=jnp.float32)
    grad_local = jnp.stack([part_real, part_imag], 0).reshape(2 * MODES * channels, channels)
    weight_grad = lax.psum_scatter(grad_local, ("dp", "dom"), scatter_dimension=0, tiled=True)
    inner = "fco,slof->slcf"
    input_real = jnp.einsum(
        inner, weight_real, grad_real, preferred_element_type=jnp.float32
    ) + jnp.einsum(inner, weight_imag, grad_imag, preferred_element_type=jnp.float32)
    input_imag = jnp.einsum(
        inner, weight_real, grad_imag, preferred_element_type=jnp.float32
    ) - jnp.einsum(inner, weight_imag, grad_real, preferred_element_type=jnp.float32)
    input_lines = inverse_cells(
        input_real.astype(jnp.bfloat16), input_imag.astype(jnp.bfloat16), cosines, sines
    )
    input_rows = lax.optimization_barrier(input_lines)
    skip_back = jnp.einsum(
        "oc,soxl->scxl", skip_weight, gate_lines, preferred_element_type=jnp.float32
    )
    grad_lines = (input_rows.astype(jnp.float32) + skip_back).astype(jnp.bfloat16)
    input_grad = lax.all_to_all(grad_lines, "dom", split_axis=2, concat_axis=3, tiled=True)
    new_moment_one = beta_first * moment_one + (1.0 - beta_first) * weight_grad
    new_moment_two = beta_second * moment_two + (1.0 - beta_second) * weight_grad * weight_grad
    first_hat = new_moment_one / (1.0 - beta_first**STEP)
    second_hat = new_moment_two / (1.0 - beta_second**STEP)
    new_weight = spectral_weight - learn_rate * (
        first_hat / (jnp.sqrt(second_hat) + epsilon) + decay_rate * spectral_weight
    )
    return (input_grad, new_weight, new_moment_one, new_moment_two)


def solution(mesh):
    placed = (
        P("dp", None, "dom", None),
        P("dp", None, "dom", None),
        P(("dp", "dom"), None),
        P(("dp", "dom"), None),
        P(("dp", "dom"), None),
        P(),
        P(),
        P(),
    )
    return jax.shard_map(
        on_device,
        mesh=mesh,
        in_specs=placed,
        out_specs=(
            P("dp", None, "dom", None),
            P(("dp", "dom"), None),
            P(("dp", "dom"), None),
            P(("dp", "dom"), None),
        ),
        check_vma=False,
    )
```

profile of v0, /device:TPU:1, one launch (start us, length us, event | category | flops | bytes accessed | tf_op | source)
XLA Modules:
  0.0 1845.9 jit_solution(2929761174149622552)
XLA Ops:
  7.2 1.5 copy.68
  8.7 0.4 copy.67
  9.3 1.5 reshape.169
  10.9 12.6 all-to-all-start
  23.5 0.6 copy-done.5
  24.1 0.6 dynamic_slice.3
  24.7 0.7 compare_convert_fusion
  25.4 0.7 compare_select_fusion.1
  26.1 1322.4 %all-gather = bf16[512,4,64]{2,1,0:T(4,128)(2,1)S(1)} all-gather(bf16[1,4,64]{2,1,0:T(4,128)(2,1)S(1)} %convert_bitcast_fusion), channel_id=1, replica_groups=mesh['dp'=8,'dom'=64] {'dp','dom'}, dimensions={0}, use_global_device_ids=true | all-gather | bytes 262656 | tf_op jit(solution)/shard_map/all_gather | solution.py:113
  1348.6 0.7 reshape.170
  1350.2 0.3 copy.81
  1351.1 0.3 fusion.65
  1351.6 0.3 fusion.9
  1352.3 0.5 fusion.45
  1354.3 0.4 fusion.62
  1354.9 0.4 fusion.8
  1355.6 0.3 copy.89
  1355.9 1.0 reshape.171
  1356.9 4.6 all-to-all-start.1
  1362.4 1.1 pad_maximum_fusion.1
  1363.6 472.5 %all-reduce.3.cloned.1.call-done = f32[2048,64]{1,0:T(8,128)} async-done(((f32[2048,64]{1,0:T(8,128)}), f32[2048,64]{1,0:T(8,128)}) %all-reduce.3.cloned.1.call-update) | async-done | bytes 524304
  1836.1 1.3 multiply_subtract_fusion
  1837.4 0.3 reshape.172
  1837.9 1.1 copy.100
  (43 shorter events, 5.5 us)
Async XLA Ops:
  7.2 1344.8 %copy-start = (bf16[64,64]{1,0:T(8,128)(2,1)S(1)}, bf16[64,64]{1,0:T(8,128)(2,1)}, u32[]{:S(2)}) copy-start(bf16[64,64]{1,0:T(8,128)(2,1)} %param.13) | copy-start | bytes 24580
  7.2 1.5 copy-start.1
  10.9 1337.7 %all-to-all-start = ((bf16[64,2,2048]{2,1,0:T(2,128)(2,1)}), bf16[64,2,2048]{2,1,0:T(2,128)(2,1)S(1)}, u32[]{:S(2)}, u32[]{:S(2)}) async-start(bf16[64,2,2048]{2,1,0:T(2,128)(2,1)} %reshape.169), calls=%async_computation | async-start | bytes 1048576 | tf_op jit(solution)/shard_map/all_to_all | solution.py:34
  23.5 0.7 copy-start.5
  24.7 1.3 copy-start.2
  1351.6 0.7 copy-start.6
  1356.9 480.5 %all-to-all-start.1 = ((bf16[64,2,1024]{2,1,0:T(2,128)(2,1)}), bf16[64,2,1024]{2,1,0:T(2,128)(2,1)S(1)}, u32[]{:S(2)}, u32[]{:S(2)}) async-start(bf16[64,2,1024]{2,1,0:T(2,128)(2,1)} %reshape.171), calls=%async_computation.1 | async-start | bytes 524288 | tf_op jit(solution)/shard_map/all_to_all | solution.py:165
  1361.5 474.5 %all-reduce.3.cloned.1.call-start = ((), (), s32[]{:S(2)}) async-start(), calls=%async_computation.2 | async-start | bytes 2097152
  1363.6 472.5 %copy-start.3 = (f32[4,64]{1,0:T(4,128)S(1)}, f32[4,64]{1,0:T(4,128)}, u32[]{:S(2)}) copy-start(f32[4,64]{1,0:T(4,128)} %param.11) | copy-start | bytes 3076
  1363.6 472.5 %copy-start.4 = (f32[4,64]{1,0:T(4,128)S(1)}, f32[4,64]{1,0:T(4,128)}, u32[]{:S(2)}) copy-start(f32[4,64]{1,0:T(4,128)} %param.12) | copy-start | bytes 3076
Sparse Core Ops, SparseCore 0:
  1367.8 468.1 all-reduce.2
where the time goes:
time: 1850 us
  blocking collectives  1320 us (71%)
  waiting for transfers between devices  472 us (26%)
    all_gather x1, blocking collectives, on_device(): weight_low = lax.all_gather(weight_short, ('dp', 'dom'), axis=0, tiled=True)  1320 us
    unnamed x2, waiting for transfers between devices  472 us
  transfers between devices with their start and end apart: 3, of which 1 were waited for; matrix products, arithmetic and copies ran while one was open for 0% of the time, Pallas kernels for 0%

commit v1 on v0

--- a/solution.py
+++ b/solution.py
@@ -110,7 +110,12 @@
     )
     keep_wide = keep_modes[:, None, None, :]
     weight_short = spectral_weight.astype(jnp.bfloat16)
-    weight_low = lax.all_gather(weight_short, ("dp", "dom"), axis=0, tiled=True)
+    weight_low = jnp.concatenate(
+        lax.all_to_all(
+            jnp.stack([weight_short] * lax.axis_size(("dp", "dom")), 0), ("dp", "dom"), 0, 0
+        ),
+        0,
+    )
     weight_low = weight_low.reshape(2, MODES, channels, channels)
     weight_real = weight_low[0]
     weight_imag = weight_low[1]

time: 1850 us -> 573 us (0.31)
  blocking collectives: 1320 us -> 0 us
  waiting for transfers between devices: 472 us -> 502 us
    all_gather x1 -> x0, blocking collectives: 1320 us -> none  [on_device(): weight_low = lax.all_gather(weight_short, ('dp', 'dom'), axis=0, tiled=True)]
    all_to_all x0 -> x1, starting transfers between devices: none -> 24.3 us  [on_device(): lax.all_to_all(jnp.stack([weight_short] * lax.axis_size(('dp', 'dom')), 0...]
    all_to_all x0 -> x1, waiting for transfers between devices: none -> 21.2 us  [on_device(): lax.all_to_all(jnp.stack([weight_short] * lax.axis_size(('dp', 'dom')), 0...]
  transfers between devices with their start and end apart: 3 -> 4, of which waited for: 1 -> 3; matrix products, arithmetic and copies ran while one was open for 0% -> 1% of each run, Pallas kernels for 0% -> 0%
where the time goes in v1:
time: 573 us; the launch traced here: 572 us
  waiting for transfers between devices  502 us (88%)
  starting transfers between devices  35.1 us (6%)
  between operations  14.3 us (2%)
  local copies, waits for them, and re-layouts  10 us (2%)
  matrix products  6.03 us (1%)
    unnamed x2, waiting for transfers between devices  466 us
    all_to_all x1, starting transfers between devices, on_device(): lax.all_to_all(jnp.stack([weight_short] * lax.axis_size(('dp', 'dom')), 0...  24.3 us
    all_to_all x1, waiting for transfers between devices, on_device(): lax.all_to_all(jnp.stack([weight_short] * lax.axis_size(('dp', 'dom')), 0...  21.2 us
    all_to_all x1, waiting for transfers between devices, in_one_piece(): lax.all_to_all(both, axis, split_axis=split_dim, concat_axis=concat_dim,...  14.2 us
  transfers between devices with their start and end apart: 4, of which 3 were waited for; matrix products, arithmetic and copies ran while one was open for 1% of the time, Pallas kernels for 0%

profile of v1, /device:TPU:1, one launch (start us, length us, event | category | flops | bytes accessed | tf_op | source)
XLA Modules:
  0.0 572.3 jit_solution(4308299857893684298)
XLA Ops:
  7.2 0.7 convert_element_type.165
  8.0 1.0 reshape.166
  9.0 24.3 %all-to-all-start.1 = ((bf16[512,2,128]{2,1,0:T(2,128)(2,1)}), bf16[512,2,128]{2,1,0:T(2,128)(2,1)S(1)}, u32[]{:S(2)}, u32[]{:S(2)}) async-start(bf16[512,2,128]{2,1,0:T(2,128)(2,1)} %reshape.166), calls=%async_computation.1 | async-start | bytes 524288 | tf_op jit(solution)/shard_map/all_to_all | solution.py:114
  33.3 0.4 copy.68
  33.7 0.5 copy-done.2
  34.2 0.4 copy.67
  34.9 1.5 reshape.164
  36.4 21.2 %all-to-all-done.1 = bf16[512,2,128]{2,1,0:T(2,128)(2,1)S(1)} async-done(((bf16[512,2,128]{2,1,0:T(2,128)(2,1)}), bf16[512,2,128]{2,1,0:T(2,128)(2,1)S(1)}, u32[]{:S(2)}, u32[]{:S(2)}) %all-to-all-start.1) | async-done | bytes 262176 | tf_op jit(solution)/shard_map/all_to_all | solution.py:114
  57.7 5.3 all-to-all-start
  63.1 0.6 copy-done.6
  63.7 0.6 dynamic_slice.3
  64.3 0.6 compare_convert_fusion
  64.9 0.7 compare_select_fusion.1
  66.0 14.2 %all-to-all-done = bf16[64,2,2048]{2,1,0:T(2,128)(2,1)S(1)} async-done(((bf16[64,2,2048]{2,1,0:T(2,128)(2,1)}), bf16[64,2,2048]{2,1,0:T(2,128)(2,1)S(1)}, u32[]{:S(2)}, u32[]{:S(2)}) %all-to-all-start) | async-done | bytes 524320 | tf_op jit(solution)/shard_map/all_to_all | solution.py:34
  80.3 0.7 reshape.165
  83.9 0.5 fusion.45
  86.0 0.4 fusion.62
  86.6 0.4 fusion.8
  87.5 1.0 reshape.168
  88.5 5.4 all-to-all-start.2
  94.9 1.1 pad_maximum_fusion.1
  96.0 466.5 %all-reduce.3.cloned.1.call-done = f32[2048,64]{1,0:T(8,128)} async-done(((f32[2048,64]{1,0:T(8,128)}), f32[2048,64]{1,0:T(8,128)}) %all-reduce.3.cloned.1.call-update) | async-done | bytes 524304
  562.5 1.3 multiply_subtract_fusion
  564.3 1.1 copy.100
  (49 shorter events, 7.5 us)
Async XLA Ops:
  7.2 76.5 %copy-start = (bf16[64,64]{1,0:T(8,128)(2,1)S(1)}, bf16[64,64]{1,0:T(8,128)(2,1)}, u32[]{:S(2)}) copy-start(bf16[64,64]{1,0:T(8,128)(2,1)} %param.13) | copy-start | bytes 24580
  9.0 24.3 %copy-start.1 = (bf16[1,64,8,256]{3,2,1,0:T(8,128)(2,1)S(1)}, bf16[1,64,8,256]{3,2,1,0:T(8,128)(2,1)}, u32[]{:S(2)}) copy-start(bf16[1,64,8,256]{3,2,1,0:T(8,128)(2,1)} %param.9) | copy-start | bytes 786436
  9.0 48.7 %all-to-all-start.1 = ((bf16[512,2,128]{2,1,0:T(2,128)(2,1)}), bf16[512,2,128]{2,1,0:T(2,128)(2,1)S(1)}, u32[]{:S(2)}, u32[]{:S(2)}) async-start(bf16[512,2,128]{2,1,0:T(2,128)(2,1)} %reshape.166), calls=%async_computation.1 | async-start | bytes 524288 | tf_op jit(solution)/shard_map/all_to_all | solution.py:114
  33.3 1.0 copy-start.2
  57.7 22.6 %all-to-all-start = ((bf16[64,2,2048]{2,1,0:T(2,128)(2,1)}), bf16[64,2,2048]{2,1,0:T(2,128)(2,1)S(1)}, u32[]{:S(2)}, u32[]{:S(2)}) async-start(bf16[64,2,2048]{2,1,0:T(2,128)(2,1)} %reshape.164), calls=%async_computation | async-start | bytes 1048576 | tf_op jit(solution)/shard_map/all_to_all | solution.py:34
  63.0 0.7 copy-start.6
  83.3 0.7 copy-start.7
  88.5 475.3 %all-to-all-start.2 = ((bf16[64,2,1024]{2,1,0:T(2,128)(2,1)}), bf16[64,2,1024]{2,1,0:T(2,128)(2,1)S(1)}, u32[]{:S(2)}, u32[]{:S(2)}) async-start(bf16[64,2,1024]{2,1,0:T(2,128)(2,1)} %reshape.168), calls=%async_computation.2 | async-start | bytes 524288 | tf_op jit(solution)/shard_map/all_to_all | solution.py:170
  93.9 468.6 %all-reduce.3.cloned.1.call-start = ((), (), s32[]{:S(2)}) async-start(), calls=%async_computation.3 | async-start | bytes 2097152
  96.0 466.5 %copy-start.5 = (f32[4,64]{1,0:T(4,128)S(1)}, f32[4,64]{1,0:T(4,128)}, u32[]{:S(2)}) copy-start(f32[4,64]{1,0:T(4,128)} %param.12) | copy-start | bytes 3076
  96.0 466.5 %copy-start.3 = (f32[4,64]{1,0:T(4,128)S(1)}, f32[4,64]{1,0:T(4,128)}, u32[]{:S(2)}) copy-start(f32[4,64]{1,0:T(4,128)} %param.10) | copy-start | bytes 3076
  96.0 466.5 %copy-start.4 = (f32[4,64]{1,0:T(4,128)S(1)}, f32[4,64]{1,0:T(4,128)}, u32[]{:S(2)}) copy-start(f32[4,64]{1,0:T(4,128)} %param.11) | copy-start | bytes 3076
Sparse Core Ops, SparseCore 0:
  100.2 462.2 all-reduce.2
